TPU v7x, 512 devices: a whole 4x4x16 slice. The times are simulated.
512 devices in a mesh: layer: 4 (over x), row: 8 (over y, core), col: 16 (over z).
Axes of the slice: x: 4, y: 4, z: 16, core: 2. Of those that a mesh axis runs over, the one named last changes fastest.
Arguments:
- density: bfloat16 [8192, 8192], P('row', 'col'), may hold values from -0.125 to 0.125
- hamiltonian: bfloat16 [8192, 8192], P('row', 'col'), may hold values from -6 to 6
- density_mask: int32 [128, 128], P('row', 'col'), may hold values from 0 to 1, as said below
- hamilton_mask: int32 [128, 128], P('row', 'col'), may hold values from 0 to 1, as said below
- filter_mask: int32 [128, 128], P('row', 'col'), may hold values from 0 to 1, as said below
Outputs:
- weighted: bfloat16 [8192, 8192], P('row', 'col')
Inputs may be any that keep to these rules, and one draw needn't show every extreme that they name: `density_mask`: each entry is 0 or 1; diagonal blocks are 1. `hamilton_mask`: each entry is 0 or 1; diagonal blocks are 1. `filter_mask`: each entry is 0 or 1; diagonal blocks are 1.
All inputs are finite; a program needn't handle non-finite values.
Results may differ from a plain program's by a relative error of at most 0.005.
Values may be sent and summed in bfloat16 or wider, within the bound.
No kernel may reach another device: no remote copies, remote signals or barrier semaphores. Data moves between devices by JAX's collectives and lax.ppermute only.
A program may use at most 64 MiB of HBM per device.

v0:
```python
import jax
import jax.numpy as jnp
from jax import lax
from jax.sharding import PartitionSpec as P

BS = 64


def expand_mask(mask_blocks):
    return jnp.repeat(jnp.repeat(mask_blocks, BS, axis=0), BS, axis=1).astype(jnp.bfloat16)


def inner_rows(matrix, groups, width, layer_pos):
    pieces = []
    stride = matrix.shape[0] // groups
    for group in range(groups):
        offset = group * stride + layer_pos * width
        pieces.append(lax.dynamic_slice_in_dim(matrix, offset, width, 0))
    return jnp.concatenate(pieces, axis=0)


def local(density, hamiltonian, density_mask, hamilton_mask, filter_mask):
    layers = lax.axis_size("layer")
    layer_pos = lax.axis_index("layer")
    groups = lax.axis_size("col") // lax.axis_size("row")
    tile_rows, tile_cols = density.shape
    width = tile_cols // layers
    masked_p = density * expand_mask(density_mask)
    masked_h = hamiltonian * expand_mask(hamilton_mask)
    h_inner = lax.all_gather(
        inner_rows(masked_h, groups, width, layer_pos), "row", axis=0, tiled=True
    )
    p_share = lax.dynamic_slice_in_dim(masked_p, layer_pos * width, width, 1)
    rows = h_inner
    partial_q = jnp.dot(
        lax.all_gather(p_share, "col", axis=1, tiled=True), rows, preferred_element_type=jnp.float32
    )
    summed_q = lax.psum_scatter(partial_q, "layer", scatter_dimension=1, tiled=True)
    filter_share = lax.dynamic_slice_in_dim(filter_mask, layer_pos * (width // BS), width // BS, 1)
    product = summed_q.astype(jnp.bfloat16) * expand_mask(filter_share)
    p_inner = lax.all_gather(
        inner_rows(masked_p, groups, width, layer_pos), "row", axis=0, tiled=True
    )
    rows = p_inner
    partial_w = jnp.dot(
        lax.all_gather(product, "col", axis=1, tiled=True), rows, preferred_element_type=jnp.float32
    )
    weighted = lax.psum(partial_w, "layer").astype(jnp.bfloat16)
    return weighted


def solution(mesh):
    placed = (P("row", "col"), P("row", "col"), P("row", "col"), P("row", "col"), P("row", "col"))
    return jax.shard_map(
        local, mesh=mesh, in_specs=placed, out_specs=P("row", "col"), check_vma=False
    )
```

profile of v0, /device:TPU:32, one launch (start us, length us, event | category | flops | bytes accessed | tf_op | source)
XLA Modules:
  0.0 339.1 jit_solution(550641898857958229)
XLA Ops:
  6.5 1.6 copy.9
  8.1 0.1 broadcast_in_dim.18
  8.2 0.1 convert_element_type.40
  8.4 0.5 copy.10
  8.9 0.1 broadcast_in_dim.20
  9.0 0.1 convert_element_type.43
  9.1 0.1 bitcast_multiply_fusion.1
  9.2 0.1 bitcast_multiply_fusion
  9.3 0.1 constant_dynamic-slice_fusion.1
  9.4 0.7 pad_maximum_fusion
  10.2 0.0 all-gather.7.cloned.1.call-update
  10.2 0.0 all-gather.5.cloned.1.call-start
  10.2 0.7 constant_dynamic-slice_fusion.5
  11.0 0.0 all-gather.5.cloned.1.call-update
  11.0 0.0 reduce-scatter.2.cloned.1.call-start
  11.0 37.9 %all-gather.7.cloned.1.call-done = bf16[2048,512]{0,1:T(8,128)(2,1)} async-done(((bf16[256,512]{0,1:T(8,128)(2,1)}), bf16[2048,512]{0,1:T(8,128)(2,1)}) %all-gather.7.cloned.1.call-update) | async-done | bytes 2097168 | tf_op jit(solution)/shard_map/all_gather | solution.py:30
  48.9 81.1 %all-gather.5.cloned.1.call-done = bf16[1024,2048]{0,1:T(8,128)(2,1)} async-done(((bf16[1024,128]{0,1:T(8,128)(2,1)}), bf16[1024,2048]{0,1:T(8,128)(2,1)}) %all-gather.5.cloned.1.call-update) | async-done | bytes 4194320 | tf_op jit(solution)/shard_map/all_gather | solution.py:36
  130.0 6.5 %fusion.2 = f32[1024,512]{0,1:T(8,128)} fusion(bf16[2048,512]{0,1:T(8,128)(2,1)} %all-gather.7.cloned.1.call-done, bf16[1024,2048]{0,1:T(8,128)(2,1)} %all-gather.5.cloned.1.call-done), kind=kOutput, calls=%fused_computation.13 | convolution fusion | flops 2147483648 | bytes 8388608 | tf_op jit(solution)/shard_map/dot_general | solution.py:35
  136.5 0.0 reduce-scatter.2.cloned.1.call-update
  136.5 0.0 all-gather.11.cloned.1.call-start
  136.6 0.8 pad_maximum_fusion.1
  137.3 0.0 all-gather.11.cloned.1.call-update
  137.4 0.0 all-gather.9.cloned.1.call-start
  137.4 0.7 fusion
  138.1 0.1 broadcast_in_dim.22
  138.2 0.1 convert_element_type.47
  138.3 32.2 %reduce-scatter.2.cloned.1.call-done = f32[1024,128]{0,1:T(8,128)} async-done(((f32[1024,512]{0,1:T(8,128)}), f32[1024,128]{0,1:T(8,128)}) %reduce-scatter.2.cloned.1.call-update) | async-done | bytes 524304 | tf_op jit(solution)/shard_map/reduce_scatter | solution.py:38
  170.5 1.8 bitcast_multiply_fusion.2
  172.3 34.5 %all-gather.11.cloned.1.call-done = bf16[2048,512]{0,1:T(8,128)(2,1)} async-done(((bf16[256,512]{0,1:T(8,128)(2,1)}), bf16[2048,512]{0,1:T(8,128)(2,1)}) %all-gather.11.cloned.1.call-update) | async-done | bytes 2097168 | tf_op jit(solution)/shard_map/all_gather | solution.py:41
  206.8 80.9 %all-gather.9.cloned.1.call-done = bf16[1024,2048]{0,1:T(8,128)(2,1)} async-done(((bf16[1024,128]{0,1:T(8,128)(2,1)}), bf16[1024,2048]{0,1:T(8,128)(2,1)}) %all-gather.9.cloned.1.call-update) | async-done | bytes 4194320 | tf_op jit(solution)/shard_map/all_gather | solution.py:46
  287.7 5.2 %fusion.1 = f32[1024,512]{1,0:T(8,128)S(1)} fusion(bf16[1024,2048]{0,1:T(8,128)(2,1)} %all-gather.9.cloned.1.call-done, bf16[2048,512]{0,1:T(8,128)(2,1)} %all-gather.11.cloned.1.call-done), kind=kOutput, calls=%fused_computation.12 | convolution fusion | flops 2147483648 | bytes 8388608 | tf_op jit(solution)/shard_map/dot_general | solution.py:45
  292.9 39.7 %all-reduce.1 = bf16[1024,512]{1,0:T(8,128)(2,1)} all-reduce(f32[1024,512]{1,0:T(8,128)S(1)} %fusion.1), channel_id=1, replica_groups=mesh['layer'=4,'row'=8,'col'=16] {'layer'}, use_global_device_ids=true, to_apply=%region_1.0 | all-reduce | flops 524288 | bytes 3145728 | tf_op jit(solution)/shard_map/psum | solution.py:48
  (10 shorter events, 0.0 us)
Async XLA Ops:
  6.5 1.6 copy-start.1
  6.5 1.8 copy-start
  6.5 42.4 %all-gather.7.cloned.1.call-start = ((), (), s32[]{:S(2)}) async-start(), calls=%async_computation.2 | async-start | bytes 2359296 | tf_op jit(solution)/shard_map/all_gather | solution.py:30
  6.5 2.4 copy-start.2
  10.2 119.8 %all-gather.5.cloned.1.call-start = ((), (), s32[]{:S(2)}) async-start(), calls=%async_computation.1 | async-start | bytes 4456448 | tf_op jit(solution)/shard_map/all_gather | solution.py:36
  11.0 159.5 %reduce-scatter.2.cloned.1.call-start = ((), (), s32[]{:S(2)}) async-start(), calls=%async_computation.3 | async-start | bytes 2621440 | tf_op jit(solution)/shard_map/reduce_scatter | solution.py:38
  136.5 70.2 %all-gather.11.cloned.1.call-start = ((), (), s32[]{:S(2)}) async-start(), calls=%async_computation.5 | async-start | bytes 2359296 | tf_op jit(solution)/shard_map/all_gather | solution.py:41
  137.4 150.3 %all-gather.9.cloned.1.call-start = ((), (), s32[]{:S(2)}) async-start(), calls=%async_computation.4 | async-start | bytes 4456448 | tf_op jit(solution)/shard_map/all_gather | solution.py:46
Sparse Core Ops, SparseCore 0:
  10.3 38.5 all-gather.6
  51.0 78.9 all-gather.4
  136.6 33.7 reduce-scatter.1
  172.4 34.2 all-gather.10
  208.7 78.9 all-gather.8
where the time goes:
time: 339 us
  waiting for transfers between devices  267 us (79%)
  blocking collectives  39.7 us (12%)
  between operations  13.3 us (4%)
  matrix products  11.7 us (3%)
  other arithmetic  4.13 us (1%)
  local copies, waits for them, and re-layouts  3.51 us (1%)
    all_gather x1, waiting for transfers between devices, local(): lax.all_gather(p_share, 'col', axis=1, tiled=True)  81.1 us
    all_gather x1, waiting for transfers between devices, local(): lax.all_gather(product, 'col', axis=1, tiled=True)  80.9 us
    psum x1, blocking collectives, local(): weighted = lax.psum(partial_w, 'layer').astype(jnp.bfloat16)  39.7 us
    all_gather x1, waiting for transfers between devices, local(): lax.all_gather(inner_rows(masked_h, groups, width, layer_pos), 'row', axi...  37.9 us
    all_gather x1, waiting for transfers between devices, local(): lax.all_gather(inner_rows(masked_p, groups, width, layer_pos), 'row', axi...  34.5 us
    reduce_scatter x1, waiting for transfers between devices, local(): lax.psum_scatter(partial_q, 'layer', scatter_dimension=1, tiled=True)  32.2 us
  transfers between devices with their start and end apart: 5, of which 5 were waited for; matrix products, arithmetic and copies ran while one was open for 1% of the time, Pallas kernels for 0%

commit v1 on v0

--- a/solution.py
+++ b/solution.py
@@ -45,7 +45,7 @@
     partial_w = jnp.dot(
         lax.all_gather(product, "col", axis=1, tiled=True), rows, preferred_element_type=jnp.float32
     )
-    weighted = lax.psum(partial_w, "layer").astype(jnp.bfloat16)
+    weighted = jnp.sum(lax.all_gather(partial_w, "layer"), axis=0).astype(jnp.bfloat16)
     return weighted
 
 

time: 339 us -> 395 us (1.17)
  the two profiles are of different devices: /device:TPU:32 before, /device:TPU:1 now
where the time goes in v1:
time: 395 us
  waiting for transfers between devices  355 us (90%)
  between operations  13.6 us (3%)
  matrix products  13.1 us (3%)
  other arithmetic  9.81 us (2%)
    all_gather x1, waiting for transfers between devices, local(): lax.all_gather(partial_w, 'layer')  95.9 us
    all_gather x1, waiting for transfers between devices, local(): lax.all_gather(p_share, 'col', axis=1, tiled=True)  71.5 us
    all_gather x1, waiting for transfers between devices, local(): lax.all_gather(product, 'col', axis=1, tiled=True)  71.3 us
    reduce_scatter x1, waiting for transfers between devices, local(): lax.psum_scatter(partial_q, 'layer', scatter_dimension=1, tiled=True)  40.9 us
    all_gather x1, waiting for transfers between devices, local(): lax.all_gather(inner_rows(masked_h, groups, width, layer_pos), 'row', axi...  39.9 us
    all_gather x1, waiting for transfers between devices, local(): lax.all_gather(inner_rows(masked_p, groups, width, layer_pos), 'row', axi...  35.4 us
  transfers between devices with their start and end apart: 6, of which 6 were waited for; matrix products, arithmetic and copies ran while one was open for 1% of the time, Pallas kernels for 0%

profile of v1, /device:TPU:1, one launch (start us, length us, event | category | flops | bytes accessed | tf_op | source)
XLA Modules:
  0.0 395.2 jit_solution(17550901405232977846)
XLA Ops:
  6.5 1.6 copy.9
  8.1 0.1 broadcast_in_dim.18
  8.2 0.1 convert_element_type.40
  8.4 0.5 copy.10
  8.9 0.1 broadcast_in_dim.20
  9.0 0.1 convert_element_type.43
  9.1 0.1 bitcast_multiply_fusion.1
  9.2 0.1 bitcast_multiply_fusion
  9.3 0.1 constant_dynamic-slice_fusion.1
  9.4 0.7 pad_maximum_fusion
  10.2 0.0 all-gather.7.cloned.1.call-start
  10.2 0.7 constant_dynamic-slice_fusion.5
  11.0 0.0 all-gather.7.cloned.1.call-update
  11.0 0.0 reduce-scatter.2.cloned.1.call-start
  11.0 39.9 %all-gather.9.cloned.1.call-done = bf16[2048,512]{0,1:T(8,128)(2,1)} async-done(((bf16[256,512]{0,1:T(8,128)(2,1)}), bf16[2048,512]{0,1:T(8,128)(2,1)}) %all-gather.9.cloned.1.call-update) | async-done | bytes 2097168 | tf_op jit(solution)/shard_map/all_gather | solution.py:30
  51.0 71.5 %all-gather.7.cloned.1.call-done = bf16[1024,2048]{0,1:T(8,128)(2,1)} async-done(((bf16[1024,128]{0,1:T(8,128)(2,1)}), bf16[1024,2048]{0,1:T(8,128)(2,1)}) %all-gather.7.cloned.1.call-update) | async-done | bytes 4194320 | tf_op jit(solution)/shard_map/all_gather | solution.py:36
  122.5 6.5 %fusion.2 = f32[1024,512]{0,1:T(8,128)} fusion(bf16[2048,512]{0,1:T(8,128)(2,1)} %all-gather.9.cloned.1.call-done, bf16[1024,2048]{0,1:T(8,128)(2,1)} %all-gather.7.cloned.1.call-done), kind=kOutput, calls=%fused_computation.13 | convolution fusion | flops 2147483648 | bytes 8388608 | tf_op jit(solution)/shard_map/dot_general | solution.py:35
  129.0 0.0 reduce-scatter.2.cloned.1.call-update
  129.0 0.0 all-gather.13.cloned.1.call-start
  129.0 0.7 pad_maximum_fusion.1
  129.8 0.0 all-gather.11.cloned.1.call-start
  129.9 0.7 fusion
  130.6 0.1 broadcast_in_dim.22
  130.6 0.1 convert_element_type.47
  130.7 40.9 %reduce-scatter.2.cloned.1.call-done = f32[1024,128]{0,1:T(8,128)} async-done(((f32[1024,512]{0,1:T(8,128)}), f32[1024,128]{0,1:T(8,128)}) %reduce-scatter.2.cloned.1.call-update) | async-done | bytes 524304 | tf_op jit(solution)/shard_map/reduce_scatter | solution.py:38
  171.6 1.8 bitcast_multiply_fusion.2
  173.4 0.0 all-gather.15.cloned.1.call-start
  173.4 35.4 %all-gather.13.cloned.1.call-done = bf16[2048,512]{0,1:T(8,128)(2,1)} async-done(((bf16[256,512]{0,1:T(8,128)(2,1)}), bf16[2048,512]{0,1:T(8,128)(2,1)}) %all-gather.13.cloned.1.call-update) | async-done | bytes 2097168 | tf_op jit(solution)/shard_map/all_gather | solution.py:41
  208.8 71.3 %all-gather.11.cloned.1.call-done = bf16[1024,2048]{0,1:T(8,128)(2,1)} async-done(((bf16[1024,128]{0,1:T(8,128)(2,1)}), bf16[1024,2048]{0,1:T(8,128)(2,1)}) %all-gather.11.cloned.1.call-update) | async-done | bytes 4194320 | tf_op jit(solution)/shard_map/all_gather | solution.py:46
  280.2 6.6 %fusion.1 = f32[1024,512]{1,0:T(8,128)} fusion(bf16[1024,2048]{0,1:T(8,128)(2,1)} %all-gather.11.cloned.1.call-done, bf16[2048,512]{0,1:T(8,128)(2,1)} %all-gather.13.cloned.1.call-done), kind=kOutput, calls=%fused_computation.12 | convolution fusion | flops 2147483648 | bytes 8388608 | tf_op jit(solution)/shard_map/dot_general | solution.py:45
  286.8 95.9 %all-gather.15.cloned.1.call-done = f32[4096,512]{1,0:T(8,128)} async-done(((f32[1024,512]{1,0:T(8,128)}), f32[4096,512]{1,0:T(8,128)}) %all-gather.15.cloned.1.call-update) | async-done | bytes 8388624 | tf_op jit(solution)/shard_map/all_gather | solution.py:48
  382.7 5.7 %reduce_sum.9 = bf16[1024,512]{1,0:T(8,128)(2,1)} reduce(f32[4,1024,512]{2,1,0:T(8,128)} %bitcast.17, f32[]{:T(128)} %constant.21.clone.1), dimensions={0}, to_apply=%region_1.0 | reduce | flops 1572864 | bytes 9437188 | tf_op jit(solution)/shard_map/reduce_sum | solution.py:48
  (13 shorter events, 0.1 us)
Async XLA Ops:
  6.5 1.6 copy-start.1
  6.5 1.8 copy-start
  6.5 44.4 %all-gather.9.cloned.1.call-start = ((), (), s32[]{:S(2)}) async-start(), calls=%async_computation.2 | async-start | bytes 2359296 | tf_op jit(solution)/shard_map/all_gather | solution.py:30
  6.5 2.4 copy-start.2
  10.2 112.3 %all-gather.7.cloned.1.call-start = ((), (), s32[]{:S(2)}) async-start(), calls=%async_computation.1 | async-start | bytes 4456448 | tf_op jit(solution)/shard_map/all_gather | solution.py:36
  11.0 160.6 %reduce-scatter.2.cloned.1.call-start = ((), (), s32[]{:S(2)}) async-start(), calls=%async_computation.3 | async-start | bytes 2621440 | tf_op jit(solution)/shard_map/reduce_scatter | solution.py:38
  129.0 79.8 %all-gather.13.cloned.1.call-start = ((), (), s32[]{:S(2)}) async-start(), calls=%async_computation.5 | async-start | bytes 2359296 | tf_op jit(solution)/shard_map/all_gather | solution.py:41
  129.8 150.4 %all-gather.11.cloned.1.call-start = ((), (), s32[]{:S(2)}) async-start(), calls=%async_computation.4 | async-start | bytes 4456448 | tf_op jit(solution)/shard_map/all_gather | solution.py:46
  173.4 209.3 %all-gather.15.cloned.1.call-start = ((), (), s32[]{:S(2)}) async-start(), calls=%async_computation.6 | async-start | bytes 10485760 | tf_op jit(solution)/shard_map/all_gather | solution.py:48
Sparse Core Ops, SparseCore 0:
  10.3 40.6 all-gather.8
  53.1 69.3 all-gather.6
  129.1 42.4 reduce-scatter.1
  173.6 35.2 all-gather.12
  210.8 69.3 all-gather.10
  286.9 95.7 all-gather.14

commit v2 on v0

--- a/solution.py
+++ b/solution.py
@@ -38,8 +38,14 @@
     summed_q = lax.psum_scatter(partial_q, "layer", scatter_dimension=1, tiled=True)
     filter_share = lax.dynamic_slice_in_dim(filter_mask, layer_pos * (width // BS), width // BS, 1)
     product = summed_q.astype(jnp.bfloat16) * expand_mask(filter_share)
-    p_inner = lax.all_gather(
-        inner_rows(masked_p, groups, width, layer_pos), "row", axis=0, tiled=True
+    p_inner = jnp.concatenate(
+        lax.all_to_all(
+            jnp.stack([inner_rows(masked_p, groups, width, layer_pos)] * lax.axis_size("row")),
+            "row",
+            0,
+            0,
+        ),
+        axis=0,
     )
     rows = p_inner
     partial_w = jnp.dot(

time: 339 us -> 303 us (0.89)
  waiting for transfers between devices: 267 us -> 198 us
  blocking collectives: 39.7 us -> 71.7 us
    all_gather x1, waiting for transfers between devices: 80.9 us -> 46.3 us  [local(): lax.all_gather(product, 'col', axis=1, tiled=True)]
    all_gather x1 -> x0, waiting for transfers between devices: 34.5 us -> none  [local(): lax.all_gather(inner_rows(masked_p, groups, width, layer_pos), 'row', axi...]
    all_to_all x0 -> x1, blocking collectives: none -> 31.3 us  [local(): lax.all_to_all(jnp.stack([inner_rows(masked_p, groups, width, layer_pos)]...]
  transfers between devices with their start and end apart: 5 -> 4, of which waited for: 5 -> 4; matrix products, arithmetic and copies ran while one was open for 1% -> 1% of each run, Pallas kernels for 0% -> 0%
where the time goes in v2:
time: 303 us
  waiting for transfers between devices  198 us (65%)
  blocking collectives  71.7 us (24%)
  between operations  13.3 us (4%)
  matrix products  12.4 us (4%)
  local copies, waits for them, and re-layouts  3.84 us (1%)
  other arithmetic  3.4 us (1%)
    all_gather x1, waiting for transfers between devices, local(): lax.all_gather(p_share, 'col', axis=1, tiled=True)  81.1 us
    all_gather x1, waiting for transfers between devices, local(): lax.all_gather(product, 'col', axis=1, tiled=True)  46.3 us
    psum x1, blocking collectives, local(): weighted = lax.psum(partial_w, 'layer').astype(jnp.bfloat16)  40.4 us
    all_gather x1, waiting for transfers between devices, local(): lax.all_gather(inner_rows(masked_h, groups, width, layer_pos), 'row', axi...  37.9 us
    reduce_scatter x1, waiting for transfers between devices, local(): lax.psum_scatter(partial_q, 'layer', scatter_dimension=1, tiled=True)  33.1 us
    all_to_all x1, blocking collectives, local(): lax.all_to_all(jnp.stack([inner_rows(masked_p, groups, width, layer_pos)]...  31.3 us
    dot_general x1, matrix products, local(): jnp.dot(lax.all_gather(p_share, 'col', axis=1, tiled=True), rows, preferr...  6.5 us
  transfers between devices with their start and end apart: 4, of which 4 were waited for; matrix products, arithmetic and copies ran while one was open for 1% of the time, Pallas kernels for 0%

profile of v2, /device:TPU:32, one launch (start us, length us, event | category | flops | bytes accessed | tf_op | source)
XLA Modules:
  0.0 303.1 jit_solution(6221576494593236263)
XLA Ops:
  6.5 1.6 copy.9
  8.1 0.1 broadcast_in_dim.18
  8.2 0.1 convert_element_type.40
  8.4 0.5 copy.10
  8.9 0.1 broadcast_in_dim.20
  9.0 0.1 convert_element_type.43
  9.1 0.1 bitcast_multiply_fusion.1
  9.2 0.1 bitcast_multiply_fusion
  9.3 0.1 constant_dynamic-slice_fusion.1
  9.4 0.7 pad_maximum_fusion
  10.2 0.0 all-gather.6.cloned.1.call-update
  10.2 0.0 all-gather.4.cloned.1.call-start
  10.2 0.7 constant_dynamic-slice_fusion.5
  11.0 0.0 all-gather.4.cloned.1.call-update
  11.0 0.0 reduce-scatter.2.cloned.1.call-start
  11.0 37.9 %all-gather.6.cloned.1.call-done = bf16[2048,512]{0,1:T(8,128)(2,1)} async-done(((bf16[256,512]{0,1:T(8,128)(2,1)}), bf16[2048,512]{0,1:T(8,128)(2,1)}) %all-gather.6.cloned.1.call-update) | async-done | bytes 2097168 | tf_op jit(solution)/shard_map/all_gather | solution.py:30
  48.9 81.1 %all-gather.4.cloned.1.call-done = bf16[1024,2048]{0,1:T(8,128)(2,1)} async-done(((bf16[1024,128]{0,1:T(8,128)(2,1)}), bf16[1024,2048]{0,1:T(8,128)(2,1)}) %all-gather.4.cloned.1.call-update) | async-done | bytes 4194320 | tf_op jit(solution)/shard_map/all_gather | solution.py:36
  130.0 6.5 %fusion.2 = f32[1024,512]{0,1:T(8,128)} fusion(bf16[2048,512]{0,1:T(8,128)(2,1)} %all-gather.6.cloned.1.call-done, bf16[1024,2048]{0,1:T(8,128)(2,1)} %all-gather.4.cloned.1.call-done), kind=kOutput, calls=%fused_computation.13 | convolution fusion | flops 2147483648 | bytes 8388608 | tf_op jit(solution)/shard_map/dot_general | solution.py:35
  136.5 0.0 reduce-scatter.2.cloned.1.call-update
  136.5 0.0 all-gather.8.cloned.1.call-start
  136.6 0.7 fusion
  137.3 0.1 broadcast_in_dim.22
  137.4 0.1 convert_element_type.47
  137.4 33.1 %reduce-scatter.2.cloned.1.call-done = f32[1024,128]{0,1:T(8,128)} async-done(((f32[1024,512]{0,1:T(8,128)}), f32[1024,128]{0,1:T(8,128)}) %reduce-scatter.2.cloned.1.call-update) | async-done | bytes 524304 | tf_op jit(solution)/shard_map/reduce_scatter | solution.py:38
  170.5 1.8 bitcast_multiply_fusion.2
  172.3 0.0 all-gather.8.cloned.1.call-update
  172.4 0.1 copy.11
  172.5 0.2 stack.2
  172.7 31.3 %all_to_all.5 = bf16[8,256,512]{2,1,0:T(8,128)(2,1)S(1)} all-to-all(bf16[8,256,512]{2,1,0:T(8,128)(2,1)S(1)} %stack.2), channel_id=1, replica_groups=mesh['layer'=4,'row'=8,'col'=16] {'row'}, dimensions={0} | all-to-all | bytes 4194304 | tf_op jit(solution)/shard_map/all_to_all | solution.py:42
  204.0 46.3 %all-gather.8.cloned.1.call-done = bf16[1024,2048]{0,1:T(8,128)(2,1)} async-done(((bf16[1024,128]{0,1:T(8,128)(2,1)}), bf16[1024,2048]{0,1:T(8,128)(2,1)}) %all-gather.8.cloned.1.call-update) | async-done | bytes 4194320 | tf_op jit(solution)/shard_map/all_gather | solution.py:52
  250.3 5.9 %fusion.1 = f32[1024,512]{1,0:T(8,128)} fusion(bf16[1024,2048]{0,1:T(8,128)(2,1)} %all-gather.8.cloned.1.call-done, bf16[2048,512]{1,0:T(8,128)(2,1)S(1)} %bitcast.17), kind=kOutput, calls=%fused_computation.12 | convolution fusion | flops 2147483648 | bytes 8388608 | tf_op jit(solution)/shard_map/dot_general | solution.py:51
  256.2 40.4 %all-reduce.1 = bf16[1024,512]{1,0:T(8,128)(2,1)} all-reduce(f32[1024,512]{1,0:T(8,128)} %fusion.1), channel_id=1, replica_groups=mesh['layer'=4,'row'=8,'col'=16] {'layer'}, use_global_device_ids=true, to_apply=%region_1.0 | all-reduce | flops 524288 | bytes 3145728 | tf_op jit(solution)/shard_map/psum | solution.py:54
  (10 shorter events, 0.1 us)
Async XLA Ops:
  6.5 1.6 copy-start.1
  6.5 1.8 copy-start
  6.5 42.4 %all-gather.6.cloned.1.call-start = ((), (), s32[]{:S(2)}) async-start(), calls=%async_computation.3 | async-start | bytes 2359296 | tf_op jit(solution)/shard_map/all_gather | solution.py:30
  6.5 2.4 copy-start.2
  10.2 119.8 %all-gather.4.cloned.1.call-start = ((), (), s32[]{:S(2)}) async-start(), calls=%async_computation.2 | async-start | bytes 4456448 | tf_op jit(solution)/shard_map/all_gather | solution.py:36
  11.0 159.6 %reduce-scatter.2.cloned.1.call-start = ((), (), s32[]{:S(2)}) async-start(), calls=%async_computation.4 | async-start | bytes 2621440 | tf_op jit(solution)/shard_map/reduce_scatter | solution.py:38
  136.5 113.8 %all-gather.8.cloned.1.call-start = ((), (), s32[]{:S(2)}) async-start(), calls=%async_computation.5 | async-start | bytes 4456448 | tf_op jit(solution)/shard_map/all_gather | solution.py:52
Sparse Core Ops, SparseCore 0:
  10.3 38.5 all-gather.5
  51.0 78.9 all-gather.3
  136.7 33.8 reduce-scatter.1
  172.5 77.7 all-gather.7
